TPU v7x, 32 devices: a whole 2x2x4 slice. The times are simulated.
32 devices in a mesh: dp: 8 (over z, x), spatial: 4 (over y, core).
Axes of the slice: x: 2, y: 2, z: 4, core: 2. Of those that a mesh axis runs over, the one named last changes fastest.
Arguments:
- fields: bfloat16 [8, 64, 128, 768], P('dp', 'spatial'), may hold values from -6 to 6
- norm_gain: float32 [768], replicated, may hold values from 0.5 to 1.5
- norm_shift: float32 [768], replicated, may hold values from -3 to 3
- first_weight: bfloat16 [2, 8, 96, 96], replicated, may hold values from -0.4375 to 0.4375
- first_bias: float32 [8, 192], replicated, may hold values from -3 to 3
- second_weight: bfloat16 [2, 8, 96, 96], replicated, may hold values from -0.4375 to 0.4375
- second_bias: float32 [8, 192], replicated, may hold values from -3 to 3
- cotangent: bfloat16 [8, 64, 128, 768], P('dp', 'spatial'), may hold values from -6 to 6
Outputs:
- block_output: bfloat16 [8, 64, 128, 768], P('dp', 'spatial')
- grad_fields: bfloat16 [8, 64, 128, 768], P('dp', 'spatial')
- grad_first: float32 [2, 8, 96, 96], replicated
- grad_first_bias: float32 [8, 192], replicated
- grad_second: float32 [2, 8, 96, 96], replicated
- grad_second_bias: float32 [8, 192], replicated
- grad_gain: float32 [768], replicated
- grad_shift: float32 [768], replicated
All inputs are finite; a program needn't handle non-finite values.
Results may differ from a plain program's by a relative error of at most 0.017.
The roundings to bfloat16 on the way count: a program that leaves them out, or rounds other values in their place, can miss the bound.
Values may be sent and summed in bfloat16 or wider, within the bound.
No kernel may reach another device: no remote copies, remote signals or barrier semaphores. Data moves between devices by JAX's collectives and lax.ppermute only.
A program may use at most 192 MiB of HBM per device.

v0:
```python
import math
import jax
import jax.numpy as jnp
from jax import lax
from jax.sharding import PartitionSpec as P

LAT = 64
LON = 128
BLOCKS = 8
BLOCK = 96
shrink_cut = 0.01
norm_epsilon = 1e-06
gelu_factor = 0.7978845608
gelu_cubic = 0.044715


def product(pattern, left_side, right_side):
    return jnp.einsum(pattern, left_side, right_side, preferred_element_type=jnp.float32)


def tables(count, mode_count, doubled):
    positions = jnp.arange(count, dtype=jnp.int32)
    orders = jnp.arange(mode_count, dtype=jnp.int32)
    phases = orders[:, None] * positions[None, :] % count
    angles = 2.0 * math.pi / count * phases.astype(jnp.float32)
    factor = jnp.ones((mode_count, 1), jnp.float32) / math.sqrt(count)
    if doubled:
        factor = factor * jnp.where(orders == 0, 1.0, 2.0).astype(jnp.float32)[:, None]
    return (
        (jnp.cos(angles) * factor).astype(jnp.bfloat16),
        (jnp.sin(angles) * factor).astype(jnp.bfloat16),
    )


def rotate(values):
    half_width = values.shape[-1] // 2
    return jnp.concatenate([values[..., half_width:], -values[..., :half_width]], axis=-1)


def along_lon(real_part, cos_table, sin_table):
    real_sum = product("bhwnp,mw->bhmnp", real_part, cos_table)
    imag_sum = -product("bhwnp,mw->bhmnp", real_part, sin_table)
    return jnp.concatenate([real_sum, imag_sum], axis=-1).astype(jnp.bfloat16)


def back_lon(spectral, cos_table, sin_table):
    half_width = spectral.shape[-1] // 2
    return product("bhmnp,mw->bhwnp", spectral[..., :half_width], cos_table) - product(
        "bhmnp,mw->bhwnp", spectral[..., half_width:], sin_table
    )


def along_lat(spectral, cos_table, sin_table):
    direct = product("kh,bhmnp->bkmnp", cos_table, spectral)
    turned = product("kh,bhmnp->bkmnp", sin_table, spectral)
    return (direct + rotate(turned)).astype(jnp.bfloat16)


def back_lat(spectral, cos_table, sin_table):
    direct = product("kh,bhmnp->bkmnp", cos_table, spectral)
    turned = product("kh,bhmnp->bkmnp", sin_table, spectral)
    return (direct - rotate(turned)).astype(jnp.bfloat16)


def real_blocks(weight):
    upper_rows = jnp.concatenate([weight[0], weight[1]], axis=-1)
    bottom = jnp.concatenate([-weight[1], weight[0]], axis=-1)
    return jnp.concatenate([upper_rows, bottom], axis=1)


def fold_blocks(gradient):
    half_width = gradient.shape[-1] // 2
    real_grad = gradient[:, :half_width, :half_width] + gradient[:, half_width:, half_width:]
    imag_grad = gradient[:, :half_width, half_width:] - gradient[:, half_width:, :half_width]
    return jnp.stack([real_grad, imag_grad])


def gelu_value(values):
    inner = jnp.tanh(gelu_factor * (values + gelu_cubic * values * values * values))
    return 0.5 * values * (1.0 + inner)


def gelu_slope(values):
    inner = jnp.tanh(gelu_factor * (values + gelu_cubic * values * values * values))
    return 0.5 * (1.0 + inner) + 0.5 * values * (1.0 - inner * inner) * gelu_factor * (
        1.0 + 3.0 * gelu_cubic * values * values
    )


def spectral_forward(transformed, first_real, first_bias, second_real, second_bias):
    hidden_pre = product("bkmnp,npq->bkmnq", transformed, first_real) + first_bias
    hidden = gelu_value(hidden_pre).astype(jnp.bfloat16)
    output_pre = product("bkmnp,npq->bkmnq", hidden, second_real) + second_bias
    shrunk = (output_pre - shrink_cut * jnp.tanh(output_pre / shrink_cut)).astype(jnp.bfloat16)
    return (hidden_pre, hidden, output_pre, shrunk)


def spectral_backward(
    transformed, hidden_pre, hidden, output_pre, grad_shrunk, first_real, second_real
):
    bend = jnp.tanh(output_pre / shrink_cut)
    grad_outpre = (grad_shrunk.astype(jnp.float32) * bend * bend).astype(jnp.bfloat16)
    grad_second = product("bkmnp,bkmnq->npq", hidden, grad_outpre)
    grad_second_bias = jnp.sum(grad_outpre.astype(jnp.float32), axis=(0, 1, 2))
    grad_hidden = product("bkmnq,npq->bkmnp", grad_outpre, second_real)
    grad_hidpre = (grad_hidden * gelu_slope(hidden_pre)).astype(jnp.bfloat16)
    grad_first = product("bkmnp,bkmnq->npq", transformed, grad_hidpre)
    grad_first_bias = jnp.sum(grad_hidpre.astype(jnp.float32), axis=(0, 1, 2))
    grad_transformed = product("bkmnq,npq->bkmnp", grad_hidpre, first_real).astype(jnp.bfloat16)
    return (grad_transformed, grad_first, grad_first_bias, grad_second, grad_second_bias)


def normalize(fields):
    values = fields.astype(jnp.float32)
    center = jnp.mean(values, axis=-1, keepdims=True)
    spread = jnp.mean((values - center) ** 2, axis=-1, keepdims=True)
    inverse_std = lax.rsqrt(spread + norm_epsilon)
    return ((values - center) * inverse_std, inverse_std)


def norm_backward(grad_scaled, normed, inverse_std, norm_gain):
    grad_normed = grad_scaled * norm_gain
    mean_grad = jnp.mean(grad_normed, axis=-1, keepdims=True)
    mean_cross = jnp.mean(grad_normed * normed, axis=-1, keepdims=True)
    return inverse_std * (grad_normed - mean_grad - normed * mean_cross)


def local(
    fields, norm_gain, norm_shift, first_weight, first_bias, second_weight, second_bias, cotangent
):
    samples, band_rows, longitudes, channels = fields.shape
    mode_count = longitudes // 2
    ahead_cos, ahead_sin = tables(longitudes, mode_count, False)
    back_cos, back_sin = tables(longitudes, mode_count, True)
    polar_cos, polar_sin = tables(LAT, LAT, False)
    first_real = real_blocks(first_weight)
    second_real = real_blocks(second_weight)
    block_shape = (samples, band_rows, longitudes, BLOCKS, BLOCK)
    normed, inverse_std = normalize(fields)
    scaled = (normed * norm_gain + norm_shift).astype(jnp.bfloat16)
    spectral = along_lon(scaled.reshape(block_shape), ahead_cos, ahead_sin)
    grad_returned = along_lon(cotangent.reshape(block_shape), back_cos, back_sin)
    columns = lax.all_to_all(spectral, "spatial", split_axis=2, concat_axis=1, tiled=True)
    transformed = along_lat(columns, polar_cos, polar_sin)
    hidden_pre, hidden, output_pre, shrunk = spectral_forward(
        transformed, first_real, first_bias, second_real, second_bias
    )
    returned = back_lat(shrunk, polar_cos, polar_sin)
    banded = lax.all_to_all(returned, "spatial", split_axis=1, concat_axis=2, tiled=True)
    mixed = back_lon(banded, back_cos, back_sin).reshape(fields.shape)
    block_output = (fields.astype(jnp.float32) + scaled.astype(jnp.float32) + mixed).astype(
        jnp.bfloat16
    )
    grad_columns = lax.all_to_all(grad_returned, "spatial", split_axis=2, concat_axis=1, tiled=True)
    grad_shrunk = along_lat(grad_columns, polar_cos, polar_sin)
    grad_transformed, g_first, g_first_bias, g_second, g_second_bias = spectral_backward(
        transformed, hidden_pre, hidden, output_pre, grad_shrunk, first_real, second_real
    )
    grad_spectral = back_lat(grad_transformed, polar_cos, polar_sin)
    grad_banded = lax.all_to_all(grad_spectral, "spatial", split_axis=1, concat_axis=2, tiled=True)
    grad_scaled = cotangent.astype(jnp.float32) + back_lon(
        grad_banded, ahead_cos, ahead_sin
    ).reshape(fields.shape)
    grad_fields = (
        cotangent.astype(jnp.float32) + norm_backward(grad_scaled, normed, inverse_std, norm_gain)
    ).astype(jnp.bfloat16)
    g_gain = jnp.sum(grad_scaled * normed, axis=(0, 1, 2))
    g_shift = jnp.sum(grad_scaled, axis=(0, 1, 2))
    terms = (
        fold_blocks(g_first),
        g_first_bias,
        fold_blocks(g_second),
        g_second_bias,
        g_gain,
        g_shift,
    )
    summed = lax.psum(
        (terms[0], terms[1], terms[2], terms[3], terms[4], terms[5]), ("dp", "spatial")
    )
    token_total = lax.axis_size("dp") * samples * LAT * LON
    scale = 1.0 / math.sqrt(token_total)
    return (
        block_output,
        grad_fields,
        summed[0] * scale,
        summed[1] * scale,
        summed[2] * scale,
        summed[3] * scale,
        summed[4] * scale,
        summed[5] * scale,
    )


def solution(mesh):
    return jax.shard_map(
        local,
        mesh=mesh,
        in_specs=(
            P("dp", "spatial", None, None),
            P(),
            P(),
            P(),
            P(),
            P(),
            P(),
            P("dp", "spatial", None, None),
        ),
        out_specs=(
            P("dp", "spatial", None, None),
            P("dp", "spatial", None, None),
            P(),
            P(),
            P(),
            P(),
            P(),
            P(),
        ),
        check_vma=False,
    )
```

profile of v0, /device:TPU:0, one launch (start us, length us, event | category | flops | bytes accessed | tf_op | source)
XLA Modules:
  0.0 488.9 jit_solution(11215165672078418992)
XLA Ops:
  17.3 4.4 copy.61
  21.7 5.1 %all-to-all-start.2 = ((bf16[1,16,64,8,192]{4,3,1,0,2:T(8,128)(2,1)}), bf16[1,16,64,8,192]{4,3,1,0,2:T(8,128)(2,1)}, u32[]{:S(2)}, u32[]{:S(2)}) async-start(bf16[1,16,64,8,192]{4,3,1,0,2:T(8,128)(2,1)} %copy.61), calls=%async_computation.2 | async-start | bytes 8388608 | tf_op jit(solution)/shard_map/all_to_all | solution.py:154
  39.8 4.5 copy.52
  44.2 31.5 %all-to-all-done.2 = bf16[1,16,64,8,192]{4,3,1,0,2:T(8,128)(2,1)} async-done(((bf16[1,16,64,8,192]{4,3,1,0,2:T(8,128)(2,1)}), bf16[1,16,64,8,192]{4,3,1,0,2:T(8,128)(2,1)}, u32[]{:S(2)}, u32[]{:S(2)}) %all-to-all-start.2) | async-done | bytes 3145760 | tf_op jit(solution)/shard_map/all_to_all | solution.py:154
  75.8 5.4 %all-to-all-start = ((bf16[1,16,64,8,192]{4,3,1,0,2:T(8,128)(2,1)}), bf16[1,16,64,8,192]{4,3,1,0,2:T(8,128)(2,1)}, u32[]{:S(2)}, u32[]{:S(2)}) async-start(bf16[1,16,64,8,192]{4,3,1,0,2:T(8,128)(2,1)} %copy.52), calls=%async_computation | async-start | bytes 8388608 | tf_op jit(solution)/shard_map/all_to_all | solution.py:143
  87.3 5.5 %copy.62 = bf16[1,16,4,16,8,192]{5,1,2,4,3,0:T(8,128)(2,1)} copy(bf16[1,16,4,16,8,192]{5,4,1,3,2,0:T(8,128)(2,1)} %bitcast.62) | data formatting | bytes 6291456 | tf_op jit(solution)/shard_map/all_to_all | solution.py:154
  92.7 36.6 %all-to-all-done = bf16[1,16,64,8,192]{4,3,1,0,2:T(8,128)(2,1)} async-done(((bf16[1,16,64,8,192]{4,3,1,0,2:T(8,128)(2,1)}), bf16[1,16,64,8,192]{4,3,1,0,2:T(8,128)(2,1)}, u32[]{:S(2)}, u32[]{:S(2)}) %all-to-all-start) | async-done | bytes 3145760 | tf_op jit(solution)/shard_map/all_to_all | solution.py:143
  132.8 4.6 convolution_bitcast_fusion
  137.4 9.3 %fusion.218 = (f32[1,64,16,8,96]{4,1,3,2,0:T(8,128)}, f32[1,64,16,8,96]{4,1,3,2,0:T(8,128)}) fusion(f32[1,64,16,8,192]{4,1,3,2,0:T(8,128)} %convolution_bitcast_fusion), kind=kLoop, calls=%fused_computation.264 | loop fusion | flops 786432 | bytes 12582912 | tf_op jit(solution)/shard_map/slice | solution.py:37
  146.7 4.9 fusion.31
  156.9 3.7 fusion.37
  166.2 4.9 fusion.217
  171.0 7.6 %fusion.9 = bf16[1,64,16,8,192]{4,1,3,2,0:T(8,128)(2,1)S(1)} fusion(f32[1,64,16,8,96]{4,1,3,2,0:T(8,128)} %get-tuple-element.39, f32[1,64,16,8,96]{4,1,3,2,0:T(8,128)} %get-tuple-element.38, f32[8,192,64,16]{1,2,3,0:T(8,128)} %copy-done.3, f32[8,192]{1,0:T(8,128)S(1)} %copy-done.21), kind=kOutput, calls=%fused_computation.17 | convolution fusion | flops 213975040 | bytes 15734784 | tf_op jit(solution)/shard_map/kh,bhmnp->bkmnp/dot_general | solution.py:18
  178.7 4.4 copy.57
  183.1 4.9 all-to-all-start.1
  187.9 6.8 %fusion.61 = f32[1,64,16,8,192]{4,1,2,3,0:T(8,128)} fusion(bf16[64,16,8,192]{3,0,2,1:T(8,128)(2,1)} %bitcast.315), kind=kOutput, calls=%fused_computation.87 | convolution fusion | flops 201392128 | bytes 9437184 | tf_op jit(solution)/shard_map/kh,bhmnp->bkmnp/dot_general | solution.py:18
  194.8 8.6 %fusion.216 = (f32[1,64,16,8,96]{4,1,2,3,0:T(8,128)S(1)}, f32[1,64,16,8,96]{4,1,2,3,0:T(8,128)}) fusion(f32[1,64,16,8,192]{4,1,2,3,0:T(8,128)} %fusion.61), kind=kLoop, calls=%fused_computation.262 | loop fusion | flops 786432 | bytes 12582912 | tf_op jit(solution)/shard_map/slice | solution.py:37
  203.4 7.0 %convert_reduce_fusion.1 = (f32[8,192]{1,0:T(8,128)}, bf16[1,64,16,8,192]{4,1,2,3,0:T(8,128)(2,1)S(1)}) fusion(f32[8,192]{1,0:T(8,128)S(1)} %copy-done.22, f32[8,192,64,16]{1,2,3,0:T(8,128)} %copy-done.3, f32[1,64,16,8,96]{4,1,2,3,0:T(8,128)} %get-tuple-element.37, f32[1,64,16,8,96]{4,1,2,3,0:T(8,128)S(1)} %get-tuple-element.36, ...), kind=kOutput, calls=%fused_computation.29 | convolution fusion | flops 218692096 | bytes 18886656 | tf_op jit(solution)/shard_map/kh,bhmnp->bkmnp/dot_general | solution.py:18
  210.4 11.2 %convert_reduce_fusion.2 = (f32[8,192]{1,0:T(8,128)}, bf16[1,64,16,8,192]{4,1,2,3,0:T(8,128)(2,1)S(1)}) fusion(f32[8,192]{1,0:T(8,128)S(1)} %copy-done.30, f32[8,192,64,16]{1,2,3,0:T(8,128)} %copy-done.7, bf16[1,64,16,8,192]{4,1,2,3,0:T(8,128)(2,1)S(1)} %get-tuple-element.55, bf16[8,96,96]{2,1,0:T(8,128)(2,1)S(1)} %copy-done.18, ...), kind=kOutput, calls=%fused_computation.30 | convolution fusion | flops 640940544 | bytes 13037568 | tf_op jit(solution)/shard_map/bkmnq,npq->bkmnp/dot_general | solution.py:18
  223.7 4.6 fusion.58
  228.3 9.2 %fusion.215 = (f32[1,64,16,8,96]{4,1,3,2,0:T(8,128)}, f32[1,64,16,8,96]{4,1,3,2,0:T(8,128)}) fusion(f32[1,64,16,8,192]{4,1,3,2,0:T(8,128)} %fusion.58), kind=kLoop, calls=%fused_computation.261 | loop fusion | flops 786432 | bytes 12582912 | tf_op jit(solution)/shard_map/slice | solution.py:37
  237.5 4.8 fusion.11
  242.4 4.4 copy.67
  246.8 3.7 fusion.76
  251.5 4.4 fusion.79
  255.9 4.8 all-to-all-start.3
  266.0 136.6 %all-reduce.4.cloned.1.call-done = (f32[2,8,96,96]{3,2,1,0:T(8,128)}, f32[2,8,96,96]{3,2,1,0:T(8,128)}) async-done(((f32[2,8,96,96]{3,2,1,0:T(8,128)}, f32[2,8,96,96]{3,2,1,0:T(8,128)}), (f32[2,8,96,96]{3,2,1,0:T(8,128)}, f32[2,8,96,96]{3,2,1,0:T(8,128)})) %all-reduce.4.cloned.1.call-update) | async-done | bytes 1179664 | tf_op jit(solution)/shard_map/psum | solution.py:177
  410.1 5.7 %convolution_subtract_fusion.1 = f32[128,16,8,96]{0,3,2,1:T(8,128)} fusion(f32[128,16,8,96]{0,3,2,1:T(8,128)S(1)} %fusion.73, bf16[1,16,64,8,192]{4,2,3,1,0:T(8,128)(2,1)S(1)} %bitcast.326, f32[64]{0:T(128)S(1)} %copy-done.28), kind=kOutput, calls=%fused_computation.90 | convolution fusion | flops 203030528 | bytes 14680576 | tf_op jit(solution)/shard_map/bhmnp,mw->bhwnp/dot_general | solution.py:18
  423.2 4.4 fusion.25
  427.6 6.1 %fusion.27 = (bf16[1,16,128,768]{2,3,1,0:T(8,128)(2,1)}, bf16[1,16,128,768]{2,3,1,0:T(8,128)(2,1)}) fusion(bf16[1,16,128,768]{2,3,1,0:T(8,128)(2,1)S(1)} %copy.51, bf16[1,16,128,768]{2,3,1,0:T(8,128)(2,1)S(1)} %copy-done.1, f32[16,128]{1,0:T(8,128)S(1)} %get-tuple-element.56, f32[16,128]{1,0:T(8,128)S(1)} %get-tuple-element.57, f32[768]{0:T(1024)S(1)} %copy-done.20, ...), kind=kLoop, calls=%fused_computation.47 | loop fusion | flops 29884416 | bytes 25204736 | tf_op jit(solution)/shard_map/convert_element_type | solution.py:166
  433.7 4.8 copy.71
  441.3 39.4 %all-reduce = (f32[8,192]{1,0:T(8,128)S(1)}, f32[8,192]{1,0:T(8,128)S(1)}, f32[768]{0:T(1024)S(1)}, f32[768]{0:T(1024)S(1)}) all-reduce(f32[8,192]{1,0:T(8,128)S(1)} %copy-done.26, f32[8,192]{1,0:T(8,128)S(1)} %copy-done.23, f32[768]{0:T(1024)S(1)} %get-tuple-element.24, ...), channel_id=1, replica_groups=mesh['dp'=8,'spatial'=4] {'dp','spatial'}, use_global_device_ids=true, to_apply=%region_6.7 | all-reduce | flops 4608 | bytes 36864 | tf_op jit(solution)/shard_map/psum | solution.py:177
  (112 shorter events, 70.3 us)
Async XLA Ops:
  7.2 5.9 %copy-start.27 = (f32[64]{0:T(128)}, f32[64]{0:T(128)S(1)}, u32[]{:S(2)}) copy-start(f32[64]{0:T(128)S(1)} %fusion.123) | copy-start | bytes 772
  10.7 4.8 copy-start
  21.7 54.1 %all-to-all-start.2 = ((bf16[1,16,64,8,192]{4,3,1,0,2:T(8,128)(2,1)}), bf16[1,16,64,8,192]{4,3,1,0,2:T(8,128)(2,1)}, u32[]{:S(2)}, u32[]{:S(2)}) async-start(bf16[1,16,64,8,192]{4,3,1,0,2:T(8,128)(2,1)} %copy.61), calls=%async_computation.2 | async-start | bytes 8388608 | tf_op jit(solution)/shard_map/all_to_all | solution.py:154
  75.8 53.6 %all-to-all-start = ((bf16[1,16,64,8,192]{4,3,1,0,2:T(8,128)(2,1)}), bf16[1,16,64,8,192]{4,3,1,0,2:T(8,128)(2,1)}, u32[]{:S(2)}, u32[]{:S(2)}) async-start(bf16[1,16,64,8,192]{4,3,1,0,2:T(8,128)(2,1)} %copy.52), calls=%async_computation | async-start | bytes 8388608 | tf_op jit(solution)/shard_map/all_to_all | solution.py:143
  146.7 4.9 %copy-start.11 = (bf16[8,96,96]{2,1,0:T(8,128)(2,1)S(1)}, bf16[8,96,96]{2,1,0:T(8,128)(2,1)}, u32[]{:S(2)}) copy-start(bf16[8,96,96]{2,1,0:T(8,128)(2,1)} %get-tuple-element.51) | copy-start | bytes 442372
  151.6 5.2 %copy-start.13 = (bf16[8,96,96]{2,1,0:T(8,128)(2,1)S(1)}, bf16[8,96,96]{2,1,0:T(8,128)(2,1)}, u32[]{:S(2)}) copy-start(bf16[8,96,96]{2,1,0:T(8,128)(2,1)} %fusion.213) | copy-start | bytes 442372
  151.6 5.2 %copy-start.15 = (bf16[8,96,96]{2,1,0:T(8,128)(2,1)S(1)}, bf16[8,96,96]{2,1,0:T(8,128)(2,1)}, u32[]{:S(2)}) copy-start(bf16[8,96,96]{2,1,0:T(8,128)(2,1)} %get-tuple-element.48) | copy-start | bytes 442372
  151.6 5.2 %copy-start.17 = (bf16[8,96,96]{2,1,0:T(8,128)(2,1)S(1)}, bf16[8,96,96]{2,1,0:T(8,128)(2,1)}, u32[]{:S(2)}) copy-start(bf16[8,96,96]{2,1,0:T(8,128)(2,1)} %get-tuple-element.49) | copy-start | bytes 442372
  151.6 5.2 %copy-start.29 = (f32[8,192]{1,0:T(8,128)S(1)}, f32[8,192]{1,0:T(8,128)}, u32[]{:S(2)}) copy-start(f32[8,192]{1,0:T(8,128)} %param.12) | copy-start | bytes 18436
  153.6 3.3 copy-start.7
  156.9 7.0 %copy-start.21 = (f32[8,192]{1,0:T(8,128)S(1)}, f32[8,192]{1,0:T(8,128)}, u32[]{:S(2)}) copy-start(f32[8,192]{1,0:T(8,128)} %param.14) | copy-start | bytes 18436
  160.6 3.2 copy-start.3
  183.1 72.8 %all-to-all-start.1 = ((bf16[1,64,16,8,192]{4,3,2,0,1:T(8,128)(2,1)}), bf16[1,64,16,8,192]{4,3,2,0,1:T(8,128)(2,1)}, u32[]{:S(2)}, u32[]{:S(2)}) async-start(bf16[1,64,16,8,192]{4,3,2,0,1:T(8,128)(2,1)} %copy.57), calls=%async_computation.1 | async-start | bytes 8388608 | tf_op jit(solution)/shard_map/all_to_all | solution.py:149
  194.8 8.6 %copy-start.2 = (bf16[1,16,4,16,8,192]{5,1,2,4,3,0:T(8,128)(2,1)S(1)}, bf16[1,16,4,16,8,192]{5,1,2,4,3,0:T(8,128)(2,1)}, u32[]{:S(2)}) copy-start(bf16[1,16,4,16,8,192]{5,1,2,4,3,0:T(8,128)(2,1)} %copy.62) | copy-start | bytes 9437188
  194.8 8.6 %copy-start.22 = (f32[8,192]{1,0:T(8,128)S(1)}, f32[8,192]{1,0:T(8,128)}, u32[]{:S(2)}) copy-start(f32[8,192]{1,0:T(8,128)} %param.14) | copy-start | bytes 18436
  203.4 7.0 %copy-start.14 = (bf16[8,96,96]{2,1,0:T(8,128)(2,1)S(1)}, bf16[8,96,96]{2,1,0:T(8,128)(2,1)}, u32[]{:S(2)}) copy-start(bf16[8,96,96]{2,1,0:T(8,128)(2,1)} %fusion.213) | copy-start | bytes 442372
  203.4 7.0 %copy-start.16 = (bf16[8,96,96]{2,1,0:T(8,128)(2,1)S(1)}, bf16[8,96,96]{2,1,0:T(8,128)(2,1)}, u32[]{:S(2)}) copy-start(bf16[8,96,96]{2,1,0:T(8,128)(2,1)} %get-tuple-element.48) | copy-start | bytes 442372
  203.4 7.0 %copy-start.18 = (bf16[8,96,96]{2,1,0:T(8,128)(2,1)S(1)}, bf16[8,96,96]{2,1,0:T(8,128)(2,1)}, u32[]{:S(2)}) copy-start(bf16[8,96,96]{2,1,0:T(8,128)(2,1)} %get-tuple-element.49) | copy-start | bytes 442372
  203.4 7.0 %copy-start.30 = (f32[8,192]{1,0:T(8,128)S(1)}, f32[8,192]{1,0:T(8,128)}, u32[]{:S(2)}) copy-start(f32[8,192]{1,0:T(8,128)} %param.12) | copy-start | bytes 18436
  210.4 11.2 %copy-start.9 = (bf16[1,64,16,8,192]{4,1,2,3,0:T(8,128)(2,1)}, bf16[1,64,16,8,192]{4,1,2,3,0:T(8,128)(2,1)S(1)}, u32[]{:S(2)}) copy-start(bf16[1,64,16,8,192]{4,1,2,3,0:T(8,128)(2,1)S(1)} %get-tuple-element.55) | copy-start | bytes 9437188
  210.4 11.2 %copy-start.12 = (bf16[8,96,96]{2,1,0:T(8,128)(2,1)S(1)}, bf16[8,96,96]{2,1,0:T(8,128)(2,1)}, u32[]{:S(2)}) copy-start(bf16[8,96,96]{2,1,0:T(8,128)(2,1)} %get-tuple-element.51) | copy-start | bytes 442372
  242.4 4.4 copy-start.5
  242.4 9.2 %slice-start.2 = ((s8[8388608]{0:T(1024)(128)(4,1)}), s8[4194304]{0:T(1024)(128)(4,1)S(1)}, s32[]{:S(2)}) async-start(s8[8388608]{0:T(1024)(128)(4,1)} %bitcast.327), calls=%async_computation.7 | async-start | bytes 8388608
  246.8 4.7 slice-start.3
  246.8 4.7 copy-start.10
  255.9 159.8 %all-to-all-start.3 = ((bf16[1,64,16,8,192]{4,3,2,0,1:T(8,128)(2,1)}), bf16[1,64,16,8,192]{4,3,2,0,1:T(8,128)(2,1)}, u32[]{:S(2)}, u32[]{:S(2)}) async-start(bf16[1,64,16,8,192]{4,3,2,0,1:T(8,128)(2,1)} %copy.67), calls=%async_computation.3 | async-start | bytes 8388608 | tf_op jit(solution)/shard_map/all_to_all | solution.py:160
  260.7 141.9 %all-reduce.4.cloned.1.call-start = ((), (), s32[]{:S(2)}) async-start(), calls=%async_computation.4 | async-start | bytes 3145728 | tf_op jit(solution)/shard_map/psum | solution.py:177
  405.2 3.4 copy-start.28
  419.2 8.4 %slice-start = ((s8[6291456]{0:T(1024)(128)(4,1)}), s8[4194304]{0:T(1024)(128)(4,1)S(1)}, s32[]{:S(2)}) async-start(s8[6291456]{0:T(1024)(128)(4,1)} %bitcast.321), calls=%async_computation.5 | async-start | bytes 8388608
  420.6 7.0 %slice-start.1 = ((s8[6291456]{0:T(1024)(128)(4,1)}), s8[2097152]{0:T(1024)(128)(4,1)S(1)}, s32[]{:S(2)}) async-start(s8[6291456]{0:T(1024)(128)(4,1)} %bitcast.321), calls=%async_computation.6 | async-start | bytes 4194304
  423.2 4.4 copy-start.25
  433.7 4.8 copy-start.6
  (8 other events, 17.4 us)
Sparse Core Ops, SparseCore 0:
  267.6 134.9 all-reduce.3
where the time goes:
time: 495 us; the launch traced here: 489 us
  waiting for transfers between devices  205 us (41%)
  matrix products  89 us (18%)
  other arithmetic  61 us (12%)
  local copies, waits for them, and re-layouts  59.3 us (12%)
  blocking collectives  39.4 us (8%)
  starting transfers between devices  20.7 us (4%)
  between operations  14.8 us (3%)
    psum x1, waiting for transfers between devices, local(): lax.psum((terms[0], terms[1], terms[2], terms[3], terms[4], terms[5]), ('...  137 us
    dot_general x22, matrix products, product(): jnp.einsum(pattern, left_side, right_side, preferred_element_type=jnp.flo...  89 us
    psum x1, blocking collectives, local(): lax.psum((terms[0], terms[1], terms[2], terms[3], terms[4], terms[5]), ('...  39.4 us
    all_to_all x1, waiting for transfers between devices, local(): lax.all_to_all(spectral, 'spatial', split_axis=2, concat_axis=1, tiled=True)  36.6 us
    slice x4, other arithmetic, rotate(): values[..., half_width:]  32 us
    all_to_all x1, waiting for transfers between devices, local(): lax.all_to_all(grad_returned, 'spatial', split_axis=2, concat_axis=1, til...  31.5 us
    unnamed x74, local copies, waits for them, and re-layouts  22.4 us
  transfers between devices with their start and end apart: 5, of which 3 were waited for; matrix products, arithmetic and copies ran while one was open for 23% of the time, Pallas kernels for 0%

commit v1 on v0

--- a/solution.py
+++ b/solution.py
@@ -12,6 +12,28 @@
 norm_epsilon = 1e-06
 gelu_factor = 0.7978845608
 gelu_cubic = 0.044715
+
+
+def in_blocks(x, dim, count):
+    before, after = (x.shape[:dim], x.shape[dim + 1 :])
+    return jnp.moveaxis(x.reshape(*before, count, -1, *after), dim, 0)
+
+
+def joined_along(tiles, dim):
+    tiles = jnp.moveaxis(tiles, 0, dim)
+    shape = tiles.shape
+    return tiles.reshape(*shape[:dim], shape[dim] * shape[dim + 1], *shape[dim + 2 :])
+
+
+def pairwise_exchange(x, axis, split_dim, concat_dim):
+    size, here = (lax.axis_size(axis), lax.axis_index(axis))
+    blocks = in_blocks(x, split_dim, size)
+    outs = [blocks[here]]
+    for step in range(1, size):
+        sent = blocks[here ^ step]
+        outs.append(lax.ppermute(sent, axis, [(i, i ^ step) for i in range(size)]))
+    blocks = jnp.stack(outs)[here ^ jnp.arange(size)]
+    return joined_along(blocks, concat_dim)
 
 
 def product(pattern, left_side, right_side):
@@ -151,7 +173,7 @@
     block_output = (fields.astype(jnp.float32) + scaled.astype(jnp.float32) + mixed).astype(
         jnp.bfloat16
     )
-    grad_columns = lax.all_to_all(grad_returned, "spatial", split_axis=2, concat_axis=1, tiled=True)
+    grad_columns = pairwise_exchange(grad_returned, "spatial", 2, 1)
     grad_shrunk = along_lat(grad_columns, polar_cos, polar_sin)
     grad_transformed, g_first, g_first_bias, g_second, g_second_bias = spectral_backward(
         transformed, hidden_pre, hidden, output_pre, grad_shrunk, first_real, second_real

time: 495 us -> 476 us (0.962)
  waiting for transfers between devices: 205 us -> 172 us
  matrix products: 89 us -> 100 us
    all_to_all x1 -> x0, waiting for transfers between devices: 31.5 us -> none  [local(): lax.all_to_all(grad_returned, 'spatial', split_axis=2, concat_axis=1, til...]
    all_to_all x1, waiting for transfers between devices: 36.6 us -> 22.4 us  [local(): lax.all_to_all(spectral, 'spatial', split_axis=2, concat_axis=1, tiled=True)]
    ppermute x0 -> x3, waiting for transfers between devices: none -> 12.7 us  [pairwise_exchange(): outs.append(lax.ppermute(sent, axis, [(i, i ^ step) for i in range(size)]))]
    dot_general x22, matrix products: 89 us -> 100 us  [product(): jnp.einsum(pattern, left_side, right_side, preferred_element_type=jnp.flo...]
    another operation x0 -> x4, local copies, waits for them, and re-layouts: none -> 5.84 us
    all_to_all x1 -> x0, local copies, waits for them, and re-layouts: 5.46 us -> none  [local(): lax.all_to_all(grad_returned, 'spatial', split_axis=2, concat_axis=1, til...]
    slice x4, other arithmetic: 32 us -> 26.7 us  [rotate(): values[..., half_width:]]
    all_to_all x1 -> x0, starting transfers between devices: 5.14 us -> none  [local(): lax.all_to_all(grad_returned, 'spatial', split_axis=2, concat_axis=1, til...]
  transfers between devices with their start and end apart: 5 -> 7, of which waited for: 3 -> 3; matrix products, arithmetic and copies ran while one was open for 23% -> 27% of each run, Pallas kernels for 0% -> 0%
where the time goes in v1:
time: 476 us; the launch traced here: 470 us
  waiting for transfers between devices  172 us (36%)
  matrix products  100 us (21%)
  other arithmetic  63.6 us (13%)
  local copies, waits for them, and re-layouts  60.9 us (13%)
  blocking collectives  39.4 us (8%)
  starting transfers between devices  18.5 us (4%)
  between operations  14.9 us (3%)
    psum x1, waiting for transfers between devices, local(): lax.psum((terms[0], terms[1], terms[2], terms[3], terms[4], terms[5]), ('...  137 us
    dot_general x22, matrix products, product(): jnp.einsum(pattern, left_side, right_side, preferred_element_type=jnp.flo...  100 us
    psum x1, blocking collectives, local(): lax.psum((terms[0], terms[1], terms[2], terms[3], terms[4], terms[5]), ('...  39.4 us
    slice x4, other arithmetic, rotate(): values[..., half_width:]  26.7 us
    unnamed x70, local copies, waits for them, and re-layouts  23 us
    all_to_all x1, waiting for transfers between devices, local(): lax.all_to_all(spectral, 'spatial', split_axis=2, concat_axis=1, tiled=True)  22.4 us
    ppermute x3, waiting for transfers between devices, pairwise_exchange(): outs.append(lax.ppermute(sent, axis, [(i, i ^ step) for i in range(size)]))  12.7 us
  transfers between devices with their start and end apart: 7, of which 3 were waited for; matrix products, arithmetic and copies ran while one was open for 27% of the time, Pallas kernels for 0%

profile of v1, /device:TPU:0, one launch (start us, length us, event | category | flops | bytes accessed | tf_op | source)
XLA Modules:
  0.0 470.1 jit_solution(11660900534651097361)
XLA Ops:
  10.7 3.8 negate_convert_fusion
  18.2 5.0 %fusion.84 = (bf16[1,16,1,16,8,192]{5,3,2,4,1,0:T(8,128)(2,1)}, bf16[1,16,1,16,8,192]{5,3,2,4,1,0:T(8,128)(2,1)S(1)}, bf16[1,16,1,16,8,192]{5,3,2,4,1,0:T(8,128)(2,1)S(1)}, bf16[1,16,1,16,8,192]{5,3,2,4,1,0:T(8,128)(2,1)S(1)}) fusion(s32[]{:T(128)S(6)} %select_n.82, bf16[1,16,4,16,8,96]{5,3,2,4,1,0:T(8,128)(2,1)} %bitcast.346, ...), kind=kLoop, calls=%fused_computation.112 | loop fusion | flops 6291456 | bytes 6291472 | tf_op jit(solution)/shard_map/concatenate | solution.py:65
  30.5 4.0 copy.55
  44.0 4.4 copy.56
  48.4 5.0 %all-to-all-start = ((bf16[1,16,64,8,192]{4,3,1,0,2:T(8,128)(2,1)}), bf16[1,16,64,8,192]{4,3,1,0,2:T(8,128)(2,1)}, u32[]{:S(2)}, u32[]{:S(2)}) async-start(bf16[1,16,64,8,192]{4,3,1,0,2:T(8,128)(2,1)} %copy.56), calls=%async_computation | async-start | bytes 8388608 | tf_op jit(solution)/shard_map/all_to_all | solution.py:165
  61.7 12.7 %collective-permute-done.1 = bf16[1,16,16,8,192]{4,3,2,1,0:T(8,128)(2,1)} collective-permute-done((bf16[1,16,16,8,192]{4,3,2,1,0:T(8,128)(2,1)}, bf16[1,16,16,8,192]{4,3,2,1,0:T(8,128)(2,1)}, u32[]{:S(2)}, u32[]{:S(2)}) %collective-permute-start.1) | collective-permute-done | bytes 786464 | tf_op jit(solution)/shard_map/ppermute | solution.py:34
  74.4 3.9 maximum_bitcast_fusion
  78.3 5.1 %gather_fusion = bf16[4,16,16,8,192]{4,3,2,1,0:T(8,128)(2,1)} fusion(bf16[4,16,16,8,192]{4,3,2,1,0:T(8,128)(2,1)} %maximum_bitcast_fusion, s32[1024]{0:T(1024)} %pad_clamp_fusion), kind=kCustom, calls=%fused_computation | custom fusion | bytes 6291472 | tf_op jit(solution)/shard_map/gather | solution.py:35
  83.5 7.7 %fusion.61 = f32[1,64,16,8,192]{4,1,2,3,0:T(8,128)S(1)} fusion(bf16[64,16,8,192]{3,2,1,0:T(8,128)(2,1)} %bitcast.333), kind=kOutput, calls=%fused_computation.96 | convolution fusion | flops 201392128 | bytes 9437184 | tf_op jit(solution)/shard_map/kh,bhmnp->bkmnp/dot_general | solution.py:40
  91.2 4.9 %fusion.220 = (f32[1,64,16,8,96]{4,1,2,3,0:T(8,128)}, f32[1,64,16,8,96]{4,1,2,3,0:T(8,128)}) fusion(f32[1,64,16,8,192]{4,1,2,3,0:T(8,128)S(1)} %fusion.61), kind=kLoop, calls=%fused_computation.281 | loop fusion | flops 786432 | bytes 12582912 | tf_op jit(solution)/shard_map/slice | solution.py:59
  96.1 22.4 %all-to-all-done = bf16[1,16,64,8,192]{4,3,1,0,2:T(8,128)(2,1)} async-done(((bf16[1,16,64,8,192]{4,3,1,0,2:T(8,128)(2,1)}), bf16[1,16,64,8,192]{4,3,1,0,2:T(8,128)(2,1)}, u32[]{:S(2)}, u32[]{:S(2)}) %all-to-all-start) | async-done | bytes 3145760 | tf_op jit(solution)/shard_map/all_to_all | solution.py:165
  121.9 4.6 convolution_bitcast_fusion
  126.5 8.5 %fusion.222 = (f32[1,64,16,8,96]{4,1,3,2,0:T(8,128)S(1)}, f32[1,64,16,8,96]{4,1,3,2,0:T(8,128)}) fusion(f32[1,64,16,8,192]{4,1,3,2,0:T(8,128)} %convolution_bitcast_fusion), kind=kLoop, calls=%fused_computation.283 | loop fusion | flops 786432 | bytes 12582912 | tf_op jit(solution)/shard_map/slice | solution.py:59
  135.1 4.4 fusion.31
  154.1 4.8 %fusion.221 = (f32[1,64,16,8,96]{4,1,3,2,0:T(8,128)}, f32[1,64,16,8,96]{4,1,3,2,0:T(8,128)}) fusion(f32[1,64,16,8,192]{4,1,3,2,0:T(8,128)S(1)} %fusion.55), kind=kLoop, calls=%fused_computation.282 | loop fusion | flops 786432 | bytes 12582912 | tf_op jit(solution)/shard_map/slice | solution.py:59
  158.9 7.5 %fusion.9 = bf16[1,64,16,8,192]{4,1,3,2,0:T(8,128)(2,1)S(1)} fusion(f32[1,64,16,8,96]{4,1,3,2,0:T(8,128)} %get-tuple-element.39, f32[1,64,16,8,96]{4,1,3,2,0:T(8,128)} %get-tuple-element.38, f32[8,192,64,16]{1,2,3,0:T(8,128)} %copy-done.2, f32[8,192]{1,0:T(8,128)S(1)} %copy-done.20), kind=kOutput, calls=%fused_computation.18 | convolution fusion | flops 213975040 | bytes 15734784 | tf_op jit(solution)/shard_map/kh,bhmnp->bkmnp/dot_general | solution.py:40
  166.4 4.4 copy.61
  170.7 5.3 %all-to-all-start.1 = ((bf16[1,64,16,8,192]{4,3,2,0,1:T(8,128)(2,1)}), bf16[1,64,16,8,192]{4,3,2,0,1:T(8,128)(2,1)}, u32[]{:S(2)}, u32[]{:S(2)}) async-start(bf16[1,64,16,8,192]{4,3,2,0,1:T(8,128)(2,1)} %copy.61), calls=%async_computation.1 | async-start | bytes 8388608 | tf_op jit(solution)/shard_map/all_to_all | solution.py:171
  176.0 16.3 %convert_reduce_fusion.1 = (f32[8,192]{1,0:T(8,128)}, bf16[1,64,16,8,192]{4,1,2,3,0:T(8,128)(2,1)S(1)}) fusion(f32[8,192]{1,0:T(8,128)} %param.14, f32[8,192,64,16]{1,2,3,0:T(8,128)} %copy-done.2, f32[1,64,16,8,96]{4,1,2,3,0:T(8,128)} %get-tuple-element.37, f32[1,64,16,8,96]{4,1,2,3,0:T(8,128)} %get-tuple-element.36, bf16[64,16,8,192]{3,2,1,0:T(8,128)(2,1)} %bitcast.334), kind=kOutput, calls=%fused_computation.30 | convolution fusion | flops 218692096 | bytes 18886656 | tf_op jit(solution)/shard_map/kh,bhmnp->bkmnp/dot_general | solution.py:40
  192.4 11.1 %convert_reduce_fusion.2 = (f32[8,192]{1,0:T(8,128)}, bf16[1,64,16,8,192]{4,1,2,3,0:T(8,128)(2,1)S(1)}) fusion(f32[8,192]{1,0:T(8,128)S(1)} %copy-done.28, f32[8,192,64,16]{1,2,3,0:T(8,128)} %copy-done.6, bf16[1,64,16,8,192]{4,1,2,3,0:T(8,128)(2,1)S(1)} %get-tuple-element.59, bf16[8,96,96]{2,1,0:T(8,128)(2,1)S(1)} %copy-done.17, ...), kind=kOutput, calls=%fused_computation.31 | convolution fusion | flops 640940544 | bytes 13037568 | tf_op jit(solution)/shard_map/bkmnq,npq->bkmnp/dot_general | solution.py:40
  205.5 4.6 fusion.58
  210.1 8.5 %fusion.219 = (f32[1,64,16,8,96]{4,1,3,2,0:T(8,128)S(1)}, f32[1,64,16,8,96]{4,1,3,2,0:T(8,128)}) fusion(f32[1,64,16,8,192]{4,1,3,2,0:T(8,128)} %fusion.58), kind=kLoop, calls=%fused_computation.280 | loop fusion | flops 786432 | bytes 12582912 | tf_op jit(solution)/shard_map/slice | solution.py:59
  218.6 4.2 fusion.11
  222.8 4.4 copy.75
  232.0 4.4 fusion.78
  236.4 4.9 %all-to-all-start.2 = ((bf16[1,64,16,8,192]{4,3,2,0,1:T(8,128)(2,1)}), bf16[1,64,16,8,192]{4,3,2,0,1:T(8,128)(2,1)}, u32[]{:S(2)}, u32[]{:S(2)}) async-start(bf16[1,64,16,8,192]{4,3,2,0,1:T(8,128)(2,1)} %copy.75), calls=%async_computation.2 | async-start | bytes 8388608 | tf_op jit(solution)/shard_map/all_to_all | solution.py:182
  246.3 137.3 %all-reduce.4.cloned.1.call-done = (f32[2,8,96,96]{3,2,1,0:T(8,128)}, f32[2,8,96,96]{3,2,1,0:T(8,128)}) async-done(((f32[2,8,96,96]{3,2,1,0:T(8,128)}, f32[2,8,96,96]{3,2,1,0:T(8,128)}), (f32[2,8,96,96]{3,2,1,0:T(8,128)}, f32[2,8,96,96]{3,2,1,0:T(8,128)})) %all-reduce.4.cloned.1.call-update) | async-done | bytes 1179664 | tf_op jit(solution)/shard_map/psum | solution.py:199
  391.2 5.6 %convolution_subtract_fusion.1 = f32[128,16,8,96]{0,3,2,1:T(8,128)} fusion(f32[128,16,8,96]{0,3,2,1:T(8,128)S(1)} %fusion.73, bf16[1,16,64,8,192]{4,2,3,1,0:T(8,128)(2,1)S(1)} %bitcast.344, f32[64]{0:T(128)S(1)} %copy-done.26), kind=kOutput, calls=%fused_computation.99 | convolution fusion | flops 203030528 | bytes 14680576 | tf_op jit(solution)/shard_map/bhmnp,mw->bhwnp/dot_general | solution.py:40
  404.2 4.5 fusion.25
  408.8 6.1 %fusion.27 = (bf16[1,16,128,768]{2,3,1,0:T(8,128)(2,1)}, bf16[1,16,128,768]{2,3,1,0:T(8,128)(2,1)}) fusion(bf16[1,16,128,768]{2,3,1,0:T(8,128)(2,1)S(1)} %copy.55, bf16[1,16,128,768]{2,3,1,0:T(8,128)(2,1)S(1)} %copy-done.1, f32[16,128]{1,0:T(8,128)S(1)} %get-tuple-element.60, f32[16,128]{1,0:T(8,128)S(1)} %get-tuple-element.61, f32[768]{0:T(1024)S(1)} %copy-done.19, ...), kind=kLoop, calls=%fused_computation.48 | loop fusion | flops 29884416 | bytes 25204736 | tf_op jit(solution)/shard_map/convert_element_type | solution.py:188
  414.8 4.8 %copy.79 = bf16[1,16,128,768]{3,2,1,0:T(8,128)(2,1)} copy(bf16[1,16,128,768]{2,3,1,0:T(8,128)(2,1)} %get-tuple-element.46) | data formatting | bytes 6291456
  422.4 39.4 %all-reduce = (f32[8,192]{1,0:T(8,128)S(1)}, f32[8,192]{1,0:T(8,128)S(1)}, f32[768]{0:T(1024)S(1)}, f32[768]{0:T(1024)S(1)}) all-reduce(f32[8,192]{1,0:T(8,128)S(1)} %copy-done.24, f32[8,192]{1,0:T(8,128)S(1)} %copy-done.21, f32[768]{0:T(1024)S(1)} %get-tuple-element.24, ...), channel_id=1, replica_groups=mesh['dp'=8,'spatial'=4] {'dp','spatial'}, use_global_device_ids=true, to_apply=%region_6.7 | all-reduce | flops 4608 | bytes 36864 | tf_op jit(solution)/shard_map/psum | solution.py:199
  (118 shorter events, 80.8 us)
Async XLA Ops:
  7.2 7.3 %copy-start.25 = (f32[64]{0:T(128)}, f32[64]{0:T(128)S(1)}, u32[]{:S(2)}) copy-start(f32[64]{0:T(128)S(1)} %fusion.142) | copy-start | bytes 772
  10.7 7.5 %copy-start = (bf16[1,16,128,768]{2,3,1,0:T(8,128)(2,1)}, bf16[1,16,128,768]{2,3,1,0:T(8,128)(2,1)S(1)}, u32[]{:S(2)}) copy-start(bf16[1,16,128,768]{2,3,1,0:T(8,128)(2,1)S(1)} %copy.63) | copy-start | bytes 9437188
  24.6 37.1 %collective-permute-start.2 = (bf16[1,16,16,8,192]{4,3,2,1,0:T(8,128)(2,1)}, bf16[1,16,16,8,192]{4,3,2,1,0:T(8,128)(2,1)}, u32[]{:S(2)}, u32[]{:S(2)}) collective-permute-start(bf16[1,16,16,8,192]{4,3,2,1,0:T(8,128)(2,1)} %bitcast.327), channel_id=1, source_target_pairs={{0,3},{1,2},{2,1},{3,0},{4,7},{5,6},{6,5},{7,4},{8,11},{9,10},{10,... | collective-permute-start | bytes 2359304 | tf_op jit(solution)/shard_map/ppermute | solution.py:34
  28.5 45.9 %collective-permute-start.1 = (bf16[1,16,16,8,192]{4,3,2,1,0:T(8,128)(2,1)}, bf16[1,16,16,8,192]{4,3,2,1,0:T(8,128)(2,1)}, u32[]{:S(2)}, u32[]{:S(2)}) collective-permute-start(bf16[1,16,16,8,192]{4,3,2,1,0:T(8,128)(2,1)} %bitcast.328), channel_id=1, source_target_pairs={{0,2},{1,3},{2,0},{3,1},{4,6},{5,7},{6,4},{7,5},{8,10},{9,11},{10,... | collective-permute-start | bytes 2359304 | tf_op jit(solution)/shard_map/ppermute | solution.py:34
  30.4 44.0 %collective-permute-start = (bf16[1,16,16,8,192]{4,3,2,1,0:T(8,128)(2,1)}, bf16[1,16,16,8,192]{4,3,2,1,0:T(8,128)(2,1)}, u32[]{:S(2)}, u32[]{:S(2)}) collective-permute-start(bf16[1,16,16,8,192]{4,3,2,1,0:T(8,128)(2,1)} %bitcast.329), channel_id=1, source_target_pairs={{0,1},{1,0},{2,3},{3,2},{4,5},{5,4},{6,7},{7,6},{8,9},{9,8},{10,11... | collective-permute-start | bytes 2359304 | tf_op jit(solution)/shard_map/ppermute | solution.py:34
  48.4 70.1 %all-to-all-start = ((bf16[1,16,64,8,192]{4,3,1,0,2:T(8,128)(2,1)}), bf16[1,16,64,8,192]{4,3,1,0,2:T(8,128)(2,1)}, u32[]{:S(2)}, u32[]{:S(2)}) async-start(bf16[1,16,64,8,192]{4,3,1,0,2:T(8,128)(2,1)} %copy.56), calls=%async_computation | async-start | bytes 8388608 | tf_op jit(solution)/shard_map/all_to_all | solution.py:165
  135.1 4.4 copy-start.10
  139.5 5.3 %copy-start.12 = (bf16[8,96,96]{2,1,0:T(8,128)(2,1)S(1)}, bf16[8,96,96]{2,1,0:T(8,128)(2,1)}, u32[]{:S(2)}) copy-start(bf16[8,96,96]{2,1,0:T(8,128)(2,1)} %fusion.217) | copy-start | bytes 442372
  139.5 5.3 %copy-start.14 = (bf16[8,96,96]{2,1,0:T(8,128)(2,1)S(1)}, bf16[8,96,96]{2,1,0:T(8,128)(2,1)}, u32[]{:S(2)}) copy-start(bf16[8,96,96]{2,1,0:T(8,128)(2,1)} %get-tuple-element.52) | copy-start | bytes 442372
  139.5 5.3 %copy-start.16 = (bf16[8,96,96]{2,1,0:T(8,128)(2,1)S(1)}, bf16[8,96,96]{2,1,0:T(8,128)(2,1)}, u32[]{:S(2)}) copy-start(bf16[8,96,96]{2,1,0:T(8,128)(2,1)} %get-tuple-element.53) | copy-start | bytes 442372
  139.5 5.3 %copy-start.27 = (f32[8,192]{1,0:T(8,128)S(1)}, f32[8,192]{1,0:T(8,128)}, u32[]{:S(2)}) copy-start(f32[8,192]{1,0:T(8,128)} %param.12) | copy-start | bytes 18436
  141.5 3.3 copy-start.6
  144.8 7.0 %copy-start.20 = (f32[8,192]{1,0:T(8,128)S(1)}, f32[8,192]{1,0:T(8,128)}, u32[]{:S(2)}) copy-start(f32[8,192]{1,0:T(8,128)} %param.14) | copy-start | bytes 18436
  148.5 3.2 copy-start.2
  170.7 65.6 %all-to-all-start.1 = ((bf16[1,64,16,8,192]{4,3,2,0,1:T(8,128)(2,1)}), bf16[1,64,16,8,192]{4,3,2,0,1:T(8,128)(2,1)}, u32[]{:S(2)}, u32[]{:S(2)}) async-start(bf16[1,64,16,8,192]{4,3,2,0,1:T(8,128)(2,1)} %copy.61), calls=%async_computation.1 | async-start | bytes 8388608 | tf_op jit(solution)/shard_map/all_to_all | solution.py:171
  176.0 16.3 %copy-start.13 = (bf16[8,96,96]{2,1,0:T(8,128)(2,1)S(1)}, bf16[8,96,96]{2,1,0:T(8,128)(2,1)}, u32[]{:S(2)}) copy-start(bf16[8,96,96]{2,1,0:T(8,128)(2,1)} %fusion.217) | copy-start | bytes 442372
  176.0 16.3 %copy-start.15 = (bf16[8,96,96]{2,1,0:T(8,128)(2,1)S(1)}, bf16[8,96,96]{2,1,0:T(8,128)(2,1)}, u32[]{:S(2)}) copy-start(bf16[8,96,96]{2,1,0:T(8,128)(2,1)} %get-tuple-element.52) | copy-start | bytes 442372
  176.0 16.3 %copy-start.17 = (bf16[8,96,96]{2,1,0:T(8,128)(2,1)S(1)}, bf16[8,96,96]{2,1,0:T(8,128)(2,1)}, u32[]{:S(2)}) copy-start(bf16[8,96,96]{2,1,0:T(8,128)(2,1)} %get-tuple-element.53) | copy-start | bytes 442372
  176.0 16.3 %copy-start.28 = (f32[8,192]{1,0:T(8,128)S(1)}, f32[8,192]{1,0:T(8,128)}, u32[]{:S(2)}) copy-start(f32[8,192]{1,0:T(8,128)} %param.12) | copy-start | bytes 18436
  192.3 11.2 %copy-start.8 = (bf16[1,64,16,8,192]{4,1,2,3,0:T(8,128)(2,1)}, bf16[1,64,16,8,192]{4,1,2,3,0:T(8,128)(2,1)S(1)}, u32[]{:S(2)}) copy-start(bf16[1,64,16,8,192]{4,1,2,3,0:T(8,128)(2,1)S(1)} %get-tuple-element.59) | copy-start | bytes 9437188
  192.4 11.2 %copy-start.11 = (bf16[8,96,96]{2,1,0:T(8,128)(2,1)S(1)}, bf16[8,96,96]{2,1,0:T(8,128)(2,1)}, u32[]{:S(2)}) copy-start(bf16[8,96,96]{2,1,0:T(8,128)(2,1)} %get-tuple-element.55) | copy-start | bytes 442372
  222.8 4.5 copy-start.4
  222.8 9.2 %slice-start.2 = ((s8[8388608]{0:T(1024)(128)(4,1)}), s8[4194304]{0:T(1024)(128)(4,1)S(1)}, s32[]{:S(2)}) async-start(s8[8388608]{0:T(1024)(128)(4,1)} %bitcast.347), calls=%async_computation.6 | async-start | bytes 8388608
  227.3 4.7 %slice-start.3 = ((s8[8388608]{0:T(1024)(128)(4,1)}), s8[4194304]{0:T(1024)(128)(4,1)S(1)}, s32[]{:S(2)}) async-start(s8[8388608]{0:T(1024)(128)(4,1)} %bitcast.347), calls=%async_computation.7 | async-start | bytes 8388608
  227.3 4.7 %copy-start.9 = (bf16[1,64,16,8,192]{4,1,2,3,0:T(8,128)(2,1)S(1)}, bf16[1,64,16,8,192]{4,1,2,3,0:T(8,128)(2,1)}, u32[]{:S(2)}) copy-start(bf16[1,64,16,8,192]{4,1,2,3,0:T(8,128)(2,1)} %copy-done.8) | copy-start | bytes 9437188
  236.4 160.4 %all-to-all-start.2 = ((bf16[1,64,16,8,192]{4,3,2,0,1:T(8,128)(2,1)}), bf16[1,64,16,8,192]{4,3,2,0,1:T(8,128)(2,1)}, u32[]{:S(2)}, u32[]{:S(2)}) async-start(bf16[1,64,16,8,192]{4,3,2,0,1:T(8,128)(2,1)} %copy.75), calls=%async_computation.2 | async-start | bytes 8388608 | tf_op jit(solution)/shard_map/all_to_all | solution.py:182
  241.3 142.4 %all-reduce.4.cloned.1.call-start = ((), (), s32[]{:S(2)}) async-start(), calls=%async_computation.3 | async-start | bytes 3145728 | tf_op jit(solution)/shard_map/psum | solution.py:199
  386.3 3.4 copy-start.26
  400.2 8.5 %slice-start = ((s8[6291456]{0:T(1024)(128)(4,1)}), s8[4194304]{0:T(1024)(128)(4,1)S(1)}, s32[]{:S(2)}) async-start(s8[6291456]{0:T(1024)(128)(4,1)} %bitcast.339), calls=%async_computation.4 | async-start | bytes 8388608
  401.6 7.1 %slice-start.1 = ((s8[6291456]{0:T(1024)(128)(4,1)}), s8[2097152]{0:T(1024)(128)(4,1)S(1)}, s32[]{:S(2)}) async-start(s8[6291456]{0:T(1024)(128)(4,1)} %bitcast.339), calls=%async_computation.5 | async-start | bytes 4194304
  404.2 4.5 copy-start.23
  414.8 4.8 %copy-start.5 = (bf16[1,16,128,768]{2,3,1,0:T(8,128)(2,1)S(1)}, bf16[1,16,128,768]{2,3,1,0:T(8,128)(2,1)}, u32[]{:S(2)}) copy-start(bf16[1,16,128,768]{2,3,1,0:T(8,128)(2,1)} %get-tuple-element.47) | copy-start | bytes 9437188
  (8 other events, 17.4 us)
Sparse Core Ops, SparseCore 0:
  248.1 135.5 all-reduce.3
